TPU v7x, 256 devices: a whole 4x4x8 slice. The times are simulated.
256 devices in a mesh: group: 32 (over x, z_lo, core), tp: 8 (over y, z_hi).
Axes of the slice: x: 4, y: 4, z: 8 (z_hi: 2, z_lo: 4; z = z_hi * 4 + z_lo), core: 2. Of those that a mesh axis runs over, the one named last changes fastest.
Arguments:
- prefill_x: bfloat16 [16384, 4096], P('group', 'tp'), may hold values from -6 to 6
- decode_x: bfloat16 [128, 4096], P('group', 'tp'), may hold values from -6 to 6
- ln_gain: float32 [4096], replicated, may hold values from 0.1 to 1.9
- ln_bias: float32 [4096], replicated, may hold values from -3 to 3
- qkv_weight: bfloat16 [4096, 3, 2048], P(None, None, 'tp'), may hold values from -0.09375 to 0.09375
- qkv_bias: float32 [3, 2048], P(None, 'tp'), may hold values from -3 to 3
- prior_cache: bfloat16 [32, 2, 512, 2048], P('group', None, None, 'tp'), may hold values from -144 to 144, as said below
- prefill_offset: int32 [32], P('group'), may hold values from 0 to 512, as said below
- home_cache: bfloat16 [128, 2, 256, 2048], P('group', None, None, 'tp'), may hold values from -144 to 144, as said below
- piece_len: int32 [128, 3], P('group'), may hold values from 0 to 1024, as said below
- side_store: bfloat16 [256, 2, 1024, 2048], P('group', None, None, 'tp'), may hold values from -144 to 144, as said below
Outputs:
- prefill_out: bfloat16 [16384, 2048], P('group', 'tp')
- decode_out: bfloat16 [128, 2048], P('group', 'tp')
Inputs may be any that keep to these rules, and one draw needn't show every extreme that they name: `prior_cache`: keys already rotated. `prefill_offset`: the largest value, 512, and 0 occur in every draw. `home_cache`: keys already rotated. `piece_len`: columns 0 and 2 are at most 1024 and reach it in every draw, 0 meaning no piece on that side; column 1 is 1 to 256 and reaches 256 in every draw. `side_store`: keys already rotated.
All inputs are finite; a program needn't handle non-finite values.
Results may differ from a plain program's by a relative error of at most 0.019.
The roundings to bfloat16 on the way count: a program that leaves them out, or rounds other values in their place, can miss the bound.
Values may be sent and summed in bfloat16 or wider, within the bound.
No kernel may reach another device: no remote copies, remote signals or barrier semaphores. Data moves between devices by JAX's collectives and lax.ppermute only.
A program may use at most 128 MiB of HBM per device.

v0:
```python
from functools import reduce
import math
import jax
import jax.numpy as jnp
from jax import lax
from jax.sharding import PartitionSpec as P

HD = 128
ROT = 32
EPS = 1e-05
NEG = -1e30


def with_halo(block, sides, width):
    for axis, dim in sides:
        count = lax.axis_size(axis)
        forward = [(i, i + 1) for i in range(count - 1)]
        forward.append((count - 1, 0))
        backward = [(target, source) for source, target in forward]
        low = lax.ppermute(
            lax.slice_in_dim(block, block.shape[dim] - width, None, axis=dim), axis, forward
        )
        high = lax.ppermute(lax.slice_in_dim(block, 0, width, axis=dim), axis, backward)
        block = jnp.concatenate([low, block, high], axis=dim)
    return block


def layer_norm(rows, gain, shift):
    rows = rows.astype(jnp.float32)
    middle = jnp.mean(rows, axis=-1, keepdims=True)
    centred = rows - middle
    spread = jnp.mean(centred * centred, axis=-1, keepdims=True)
    return (centred * lax.rsqrt(spread + EPS) * gain + shift).astype(jnp.bfloat16)


def rotate(vectors, positions):
    half = ROT // 2
    steps = jnp.arange(half, dtype=jnp.float32) * (2.0 / ROT)
    frequency = jnp.exp(-math.log(10000.0) * steps)
    angle = positions.astype(jnp.float32)[:, None] * frequency[None, :]
    cosine = jnp.cos(angle)[:, None, :]
    sine = jnp.sin(angle)[:, None, :]
    first = vectors[..., :half]
    second = vectors[..., half:ROT]
    return jnp.concatenate(
        [first * cosine - second * sine, second * cosine + first * sine, vectors[..., ROT:]],
        axis=-1,
    )


def project(normed, weight, bias, positions):
    count = normed.shape[0]
    width = weight.shape[2]
    mixed = jnp.dot(
        normed, weight.reshape(weight.shape[0], 3 * width), preferred_element_type=jnp.float32
    )
    mixed = (mixed + bias.reshape(1, 3 * width)).reshape(count, 3, width // HD, HD)
    query = rotate(mixed[:, 0], positions).astype(jnp.bfloat16)
    fresh_key = rotate(mixed[:, 1], positions).astype(jnp.bfloat16)
    fresh_value = mixed[:, 2].astype(jnp.bfloat16)
    return (query, fresh_key, fresh_value)


def attend_rows(query, keys, values, live):
    scores = jnp.einsum("qhd,khd->hqk", query, keys, preferred_element_type=jnp.float32) * (
        1.0 / math.sqrt(HD)
    )
    masked = jnp.where(live[None], scores, NEG)
    highest = jnp.max(masked, axis=2, keepdims=True)
    weights = jnp.where(live[None], jnp.exp(masked - highest), 0.0)
    total = jnp.sum(weights, axis=2)
    mixed = jnp.einsum(
        "hqk,khd->qhd", weights.astype(jnp.bfloat16), values, preferred_element_type=jnp.float32
    )
    return (mixed / jnp.transpose(total)[:, :, None]).astype(jnp.bfloat16)


def prefill_attend(query, fresh_key, fresh_value, prior, offset):
    count, heads = (query.shape[0], query.shape[1])
    capacity = prior.shape[1]
    keys = jnp.concatenate([prior[0].reshape(capacity, heads, HD), fresh_key], axis=0)
    values = jnp.concatenate([prior[1].reshape(capacity, heads, HD), fresh_value], axis=0)
    block = min(count, 512)

    def one_block(start):
        places = start + jnp.arange(block, dtype=jnp.int32)
        live = jnp.concatenate(
            [
                jnp.broadcast_to(jnp.arange(capacity)[None, :] < offset, (block, capacity)),
                jnp.arange(count)[None, :] <= places[:, None],
            ],
            axis=1,
        )
        return attend_rows(query, keys, values, live)

    starts = jnp.arange(count // block, dtype=jnp.int32) * block
    return lax.map(one_block, starts).reshape(count, heads * HD)


def piece_partial(query, keys, values, live):
    scores = jnp.einsum("hd,khd->hk", query, keys, preferred_element_type=jnp.float32) * (
        1.0 / math.sqrt(HD)
    )
    masked = jnp.where(live[None], scores, NEG)
    highest = jnp.max(masked, axis=1)
    weights = jnp.where(live[None], jnp.exp(masked - highest[:, None]), 0.0)
    total = jnp.sum(weights, axis=1)
    summed = jnp.einsum(
        "hk,khd->hd", weights.astype(jnp.bfloat16), values, preferred_element_type=jnp.float32
    )
    return (highest, total, summed)


def piece_batch(query, store, lengths):
    count, capacity = (store.shape[0], store.shape[2])
    heads = query.shape[1]
    keys = store[:, 0].reshape(count, capacity, heads, HD)
    values = store[:, 1].reshape(count, capacity, heads, HD)
    live = jnp.arange(capacity)[None, :] < lengths[:, None]
    return jax.vmap(piece_partial)(query, keys, values, live)


def home_partial(query, fresh_key, fresh_value, cache, lengths):
    count, capacity = (cache.shape[0], cache.shape[2])
    heads = query.shape[1]
    keys = jnp.concatenate(
        [cache[:, 0].reshape(count, capacity, heads, HD), fresh_key[:, None]], axis=1
    )
    values = jnp.concatenate(
        [cache[:, 1].reshape(count, capacity, heads, HD), fresh_value[:, None]], axis=1
    )
    live = jnp.concatenate(
        [jnp.arange(capacity)[None, :] < lengths[:, None], jnp.ones((count, 1), jnp.bool_)], axis=1
    )
    return jax.vmap(piece_partial)(query, keys, values, live)


def combine(parts):
    highest = reduce(jnp.maximum, [part[0] for part in parts])
    factors = [jnp.exp(part[0] - highest) for part in parts]
    upper = reduce(jnp.add, [factor[:, :, None] * part[2] for factor, part in zip(factors, parts)])
    lower = reduce(jnp.add, [factor * part[1] for factor, part in zip(factors, parts)])
    return (upper / lower[:, :, None]).astype(jnp.bfloat16)


def local(
    prefill_x,
    decode_x,
    ln_gain,
    ln_bias,
    qkv_weight,
    qkv_bias,
    prior_cache,
    prefill_offset,
    home_cache,
    piece_len,
    side_store,
):
    count = prefill_x.shape[0]
    requests = decode_x.shape[0]
    rows = jnp.concatenate([prefill_x, decode_x], axis=0)
    partner = lax.ppermute(rows, "tz", [(0, 1), (1, 0)])
    own_y = lax.all_gather(rows, "ty", axis=1, tiled=True)
    partner_y = lax.all_gather(partner, "ty", axis=1, tiled=True)
    lower = lax.axis_index("tz") == 0
    first = jnp.where(lower, own_y, partner_y).reshape(rows.shape[0], -1, 1, rows.shape[1])
    second = jnp.where(lower, partner_y, own_y).reshape(rows.shape[0], -1, 1, rows.shape[1])
    whole = jnp.concatenate([first, second], axis=2).reshape(rows.shape[0], -1)
    normed = layer_norm(whole, ln_gain, ln_bias)
    positions = jnp.concatenate(
        [
            prefill_offset[0] + jnp.arange(count, dtype=jnp.int32),
            piece_len[:, 0] + piece_len[:, 1] + piece_len[:, 2],
        ],
        axis=0,
    )
    query, fresh_key, fresh_value = project(normed, qkv_weight, qkv_bias, positions)
    own_query = query[count:]
    home_parts = home_partial(
        own_query, fresh_key[count:], fresh_value[count:], home_cache, piece_len[:, 1]
    )
    groups = lax.axis_size("group")
    forward = [(i, (i + 1) % groups) for i in range(groups)]
    backward = [((i + 1) % groups, i) for i in range(groups)]
    heads = own_query.shape[1]

    def ask(lengths, pairs):
        packed = jnp.concatenate(
            [
                own_query.astype(jnp.float32).reshape(requests, -1),
                lengths[:, None].astype(jnp.float32),
            ],
            axis=1,
        )
        got = lax.ppermute(packed, "group", pairs)
        return (
            got[:, :-1].reshape(own_query.shape).astype(own_query.dtype),
            got[:, -1].astype(jnp.int32),
        )

    def answer(parts, pairs):
        highest, total, summed = parts
        packed = jnp.concatenate([summed, highest[:, :, None], total[:, :, None]], axis=2)
        got = lax.ppermute(packed, "group", pairs)
        return (got[:, :, HD], got[:, :, HD + 1], got[:, :, :HD])

    prev_query, prev_len = ask(piece_len[:, 2], forward)
    next_query, next_len = ask(piece_len[:, 0], backward)
    right_parts = answer(piece_batch(prev_query, side_store[:requests], prev_len), backward)
    left_parts = answer(piece_batch(next_query, side_store[requests:], next_len), forward)
    prefill_out = prefill_attend(
        query[:count], fresh_key[:count], fresh_value[:count], prior_cache[0], prefill_offset[0]
    )
    decode_out = combine([left_parts, home_parts, right_parts]).reshape(requests, -1)
    return (prefill_out, decode_out)


def solution(mesh):
    devices = mesh.devices.reshape(mesh.devices.shape[0], -1, 2)
    split = jax.sharding.Mesh(devices, ("group", "ty", "tz"))
    tp = ("ty", "tz")
    inner = jax.shard_map(
        local,
        mesh=split,
        in_specs=(
            P("group", tp),
            P("group", tp),
            P(),
            P(),
            P(None, None, tp),
            P(None, tp),
            P("group", None, None, tp),
            P("group"),
            P("group", None, None, tp),
            P("group", None),
            P("group", None, None, tp),
        ),
        out_specs=(P("group", tp), P("group", tp)),
        check_vma=False,
    )
    return inner
```

profile of v0, /device:TPU:8, one launch (start us, length us, event | category | flops | bytes accessed | tf_op | source)
XLA Modules:
  0.0 197.1 jit_solution(9359004009411949456)
XLA Ops:
  7.2 1.1 constant_dynamic-update-slice_fusion.1
  8.3 0.7 constant_dynamic-update-slice_fusion
  9.0 0.8 copy-done.1
  9.9 7.3 %collective-permute-start = (bf16[516,512]{1,0:T(8,128)(2,1)}, bf16[516,512]{1,0:T(8,128)(2,1)S(1)}, u32[]{:S(2)}, u32[]{:S(2)}) collective-permute-start(bf16[516,512]{1,0:T(8,128)(2,1)} %copy-done.1), channel_id=1, source_target_pairs={{0,1},{1,0},{2,3},{3,2},{4,5},{5,4},{6,7},{7,6},{8,9},{9,8},{10,11... | collective-permute-start | bytes 1585160 | tf_op jit(solution)/shard_map/ppermute | solution.py:162
  17.1 14.6 %collective-permute-done = bf16[516,512]{1,0:T(8,128)(2,1)S(1)} collective-permute-done((bf16[516,512]{1,0:T(8,128)(2,1)}, bf16[516,512]{1,0:T(8,128)(2,1)S(1)}, u32[]{:S(2)}, u32[]{:S(2)}) %collective-permute-start) | collective-permute-done | bytes 528416 | tf_op jit(solution)/shard_map/ppermute | solution.py:162
  31.7 0.8 copy-done.4
  32.5 0.7 add.81
  33.3 0.7 mul.188
  34.0 8.8 %copy.95 = bf16[4096,3,256]{0,2,1:T(8,128)(2,1)} copy(bf16[4096,3,256]{2,0,1:T(8,128)(2,1)} %param.15) | data formatting | bytes 12582912 | tf_op args[4]
  43.6 0.2 slice_convert_fusion.7
  43.8 0.2 multiply_cosine_fusion
  44.0 0.1 copy.99
  44.2 0.8 copy.98
  45.2 0.8 copy.102
  46.0 0.8 copy.92
  46.9 5.7 %fusion.76 = (bf16[4,1,1024,256]{3,2,1,0:T(8,128)(2,1)S(1)}, bf16[4,1,1024,256]{3,2,1,0:T(8,128)(2,1)}, bf16[4,1,1024,256]{3,2,1,0:T(8,128)(2,1)}, bf16[4,1,1024,256]{3,2,1,0:T(8,128)(2,1)}) fusion(bf16[8,2,1024,256]{3,2,1,0:T(8,128)(2,1)} %param.21), kind=kLoop, calls=%fused_computation.136 | loop fusion | bytes 16777216 | tf_op jit(solution)/shard_map/slice | solution.py:118
  52.6 4.0 %copy.126 = bf16[4,1,1024,256]{2,3,0,1:T(8,128)(2,1)} copy(bf16[4,1,1024,256]{3,2,1,0:T(8,128)(2,1)} %get-tuple-element.43) | data formatting | bytes 4194304 | tf_op jit(solution)/shard_map/reshape;squeeze | solution.py:117
  56.6 4.0 %reshape_squeeze.30 = bf16[4,1024,2,128]{3,2,1,0:T(2,128)(2,1)} reshape(bf16[4,1,1024,256]{3,2,1,0:T(8,128)(2,1)} %get-tuple-element.42) | data formatting | bytes 4194304 | tf_op jit(solution)/shard_map/reshape;squeeze | solution.py:118
  60.5 2.1 %fusion.78 = (bf16[4,1,256,256]{3,2,1,0:T(8,128)(2,1)S(1)}, bf16[4,1,256,256]{3,2,1,0:T(8,128)(2,1)}) fusion(bf16[4,2,256,256]{3,2,1,0:T(8,128)(2,1)} %param.19), kind=kLoop, calls=%fused_computation.138 | loop fusion | bytes 2097152 | tf_op jit(solution)/shard_map/slice | solution.py:127
  62.7 1.2 reshape_squeeze.31
  63.8 1.0 reshape_squeeze.28
  64.8 4.0 %copy.125 = bf16[4,1,1024,256]{2,3,0,1:T(8,128)(2,1)} copy(bf16[4,1,1024,256]{3,2,1,0:T(8,128)(2,1)} %get-tuple-element.41) | data formatting | bytes 4194304 | tf_op jit(solution)/shard_map/reshape;squeeze | solution.py:117
  68.8 2.1 %reshape_squeeze.27 = bf16[4,1024,2,128]{3,2,1,0:T(2,128)(2,1)} reshape(bf16[4,1,1024,256]{3,2,1,0:T(8,128)(2,1)S(1)} %get-tuple-element.40) | data formatting | bytes 4194304 | tf_op jit(solution)/shard_map/reshape;squeeze | solution.py:118
  71.1 1.0 pad_add_fusion
  72.1 9.0 %all-gather.5.cloned.1.call-done = bf16[516,2048]{1,0:T(8,128)(2,1)} async-done(((bf16[516,512]{1,0:T(8,128)(2,1)}), bf16[516,2048]{1,0:T(8,128)(2,1)}) %all-gather.5.cloned.1.call-update) | async-done | bytes 2113552 | tf_op jit(solution)/shard_map/all_gather | solution.py:164
  81.1 3.9 %broadcast_select_fusion.1 = (bf16[516,2048]{1,0:T(8,128)(2,1)S(1)}, bf16[516,2048]{1,0:T(8,128)(2,1)}) fusion(bf16[516,2048]{1,0:T(8,128)(2,1)} %all-gather.3.cloned.1.call-done, bf16[516,2048]{1,0:T(8,128)(2,1)} %all-gather.5.cloned.1.call-done, pred[]{:T(512)S(6)} %eq.3), kind=kLoop, calls=%fused_computation.14 | loop fusion | flops 2113536 | bytes 8454145 | tf_op jit(solution)/shard_map/jit(_where)/select_n | solution.py:166
  85.0 12.5 %reshape.299 = bf16[516,4,1,512]{3,2,1,0:T(2,128)(2,1)} reshape(bf16[516,2048]{1,0:T(8,128)(2,1)} %get-tuple-element.45) | data formatting | bytes 4227072 | tf_op jit(solution)/shard_map/reshape | solution.py:167
  97.5 5.4 %reshape.298 = bf16[516,4,1,512]{3,2,1,0:T(2,128)(2,1)} reshape(bf16[516,2048]{1,0:T(8,128)(2,1)S(1)} %get-tuple-element.44) | data formatting | bytes 4227072 | tf_op jit(solution)/shard_map/reshape | solution.py:166
  102.9 14.9 %convert_reduce_fusion = (f32[516]{0:T(1024)S(1)}, bf16[516,4,2,512]{3,2,1,0:T(2,128)(2,1)S(1)}) fusion(bf16[516,4,1,512]{3,2,1,0:T(2,128)(2,1)} %reshape.299, bf16[516,4,1,512]{3,2,1,0:T(2,128)(2,1)} %reshape.298), kind=kLoop, calls=%fused_computation.2 | loop fusion | flops 12680700 | bytes 8456208 | tf_op jit(solution)/shard_map/reduce_sum | solution.py:30
  117.8 6.1 %fusion.3 = f32[516]{0:T(1024)S(1)} fusion(bf16[516,4,2,512]{3,2,1,0:T(2,128)(2,1)S(1)} %get-tuple-element.39, f32[516]{0:T(1024)S(1)} %broadcast_multiply_fusion), kind=kLoop, calls=%fused_computation.5 | loop fusion | flops 8453628 | bytes 4231200 | tf_op jit(solution)/shard_map/reduce_sum | solution.py:32
  123.9 8.8 %fusion.6 = bf16[516,4,2,512]{3,2,1,0:T(2,128)(2,1)} fusion(bf16[516,4,2,512]{3,2,1,0:T(2,128)(2,1)S(1)} %get-tuple-element.39, f32[516]{0:T(1024)S(1)} %add_rsqrt_fusion, f32[516]{0:T(1024)S(1)} %broadcast_multiply_fusion, f32[4,2,512]{2,1,0:T(2,128)S(1)} %add.81, f32[4,2,512]{2,1,0:T(2,128)S(1)} %mul.188), kind=kLoop, calls=%fused_computation.8 | loop fusion | flops 12681216 | bytes 8491040 | tf_op jit(solution)/shard_map/convert_element_type | solution.py:33
  132.7 10.6 %convert_element_type.82 = bf16[516,4096]{1,0:T(8,128)(2,1)} reshape(bf16[516,4,2,512]{3,2,1,0:T(2,128)(2,1)} %fusion.6) | data formatting | bytes 8454144 | tf_op jit(solution)/shard_map/convert_element_type | solution.py:33
  143.3 8.8 %convolution_add_fusion = f32[516,768]{1,0:T(8,128)} fusion(bf16[516,4096]{1,0:T(8,128)(2,1)} %convert_element_type.82, bf16[4096,768]{0,1:T(8,128)(2,1)} %bitcast.118, f32[768]{0:T(1024)S(1)} %add.84), kind=kOutput, calls=%fused_computation.25 | convolution fusion | flops 3246787584 | bytes 12106752 | tf_op jit(solution)/shard_map/dot_general | solution.py:54
  152.1 2.1 %reshape.279 = f32[516,3,2,128]{3,2,1,0:T(2,128)S(1)} reshape(f32[516,768]{1,0:T(8,128)} %convolution_add_fusion) | data formatting | bytes 3170304 | tf_op jit(solution)/shard_map/reshape | solution.py:57
  154.2 0.4 fusion.77
  154.5 2.2 %copy.96 = bf16[516,3,2,128]{0,3,2,1:T(8,128)(2,1)} copy(f32[516,3,2,128]{3,2,1,0:T(2,128)S(1)} %reshape.279) | data formatting | bytes 2377728 | tf_op jit(solution)/shard_map/reshape | solution.py:57
  157.1 1.4 subtract_convert_fusion.1
  158.6 0.3 pad_maximum_fusion.3
  158.9 1.0 slice_bitcast_fusion
  160.0 0.8 slice.182
  160.8 0.3 pad_maximum_fusion.4
  161.4 5.7 %collective-permute-start.1 = (f32[4,257]{1,0:T(4,128)S(1)}, f32[4,257]{1,0:T(4,128)S(1)}, u32[]{:S(2)}, u32[]{:S(2)}) collective-permute-start(f32[4,257]{1,0:T(4,128)S(1)} %get-tuple-element.68), channel_id=1, source_target_pairs={{8,0},{16,8},{24,16},{32,24},{40,32},{48,40},{56,48},{64,56},{72,6... | collective-permute-start | bytes 12344 | tf_op jit(solution)/shard_map/ppermute | solution.py:195
  167.1 0.7 fusion.33
  167.8 2.4 %fusion.80 = (f32[2,512]{1,0:T(2,128)S(1)}, bf16[2,512,1024]{2,1,0:T(8,128)(2,1)S(1)}) fusion(f32[2,512,1024]{2,1,0:T(8,128)S(1)} %fusion.33, pred[512,1024]{1,0:T(8,128)(4,1)S(1)} %copy-done.5), kind=kOutput, calls=%fused_computation.140 | output fusion | flops 8389631 | bytes 6819840 | tf_op jit(solution)/shard_map/while/body/eval_jaxpr/sub | solution.py:70
  170.2 0.7 pad_maximum_fusion.2
  170.9 0.7 pad_maximum_fusion.1
  171.6 0.3 fusion.28
  171.9 0.8 fusion.23
  172.8 0.2 fusion.56
  173.2 2.0 %fusion.82 = f32[4,2,1,1024]{3,2,1,0:T(1,128)S(1)} fusion(bf16[4,2,128,1]{2,3,1,0:T(2,128)(2,1)S(1)} %reshape.303, bf16[4,1024,2,128]{1,3,2,0:T(8,128)(2,1)} %bitcast.117), kind=kOutput, calls=%fused_computation.142 | convolution fusion | flops 2097152 | bytes 2131968 | tf_op jit(solution)/shard_map/vmap(hd,khd->hk)/dot_general | solution.py:101
  175.2 0.2 fusion.50
  175.4 2.0 %fusion.8 = f32[4,2,1,128]{3,2,1,0:T(1,128)S(1)} fusion(bf16[4,1024,2,128]{3,2,1,0:T(2,128)(2,1)} %reshape_squeeze.30, bf16[4,2,1024,1]{2,0,1,3:T(4,128)(2,1)S(1)} %get-tuple-element.62), kind=kOutput, calls=%fused_computation.15 | convolution fusion | flops 2097152 | bytes 2117632 | tf_op jit(solution)/shard_map/vmap(hk,khd->hd)/dot_general | solution.py:108
  177.4 0.2 copy.121
  177.7 0.2 collective-permute-start.4
  178.1 0.4 fusion.81
  178.6 0.2 fusion.51
  178.8 2.0 %fusion.10 = f32[4,2,1,128]{3,2,1,0:T(1,128)S(1)} fusion(bf16[4,1024,2,128]{3,2,1,0:T(2,128)(2,1)} %reshape_squeeze.27, bf16[4,2,1024,1]{2,0,1,3:T(4,128)(2,1)S(1)} %get-tuple-element.60), kind=kOutput, calls=%fused_computation.17 | convolution fusion | flops 2097152 | bytes 2117632 | tf_op jit(solution)/shard_map/vmap(hk,khd->hd)/dot_general | solution.py:108
  180.8 0.2 copy.112
  181.0 0.5 collective-permute-start.2
  181.5 0.2 fusion.26
  181.7 0.9 copy.106
  182.5 0.2 copy.124
  182.7 6.7 %collective-permute-done.2 = f32[4,2,130]{0,1,2:T(2,128)S(1)} collective-permute-done((f32[4,2,130]{0,1,2:T(2,128)S(1)}, f32[4,2,130]{0,1,2:T(2,128)S(1)}, u32[]{:S(2)}, u32[]{:S(2)}) %collective-permute-start.2) | collective-permute-done | bytes 4192 | tf_op jit(solution)/shard_map/ppermute | solution.py:204
  189.6 0.7 copy.105
  (65 shorter events, 2.3 us)
Async XLA Ops:
  7.2 64.9 %all-gather.3.cloned.1.call-start = ((), (), s32[]{:S(2)}) async-start(), calls=%async_computation | async-start | bytes 2662400 | tf_op jit(solution)/shard_map/all_gather | solution.py:163
  9.0 0.8 copy-start.1
  9.8 71.3 %all-gather.5.cloned.1.call-start = ((), (), s32[]{:S(2)}) async-start(), calls=%async_computation.1 | async-start | bytes 2662400 | tf_op jit(solution)/shard_map/all_gather | solution.py:164
  9.9 21.8 %collective-permute-start = (bf16[516,512]{1,0:T(8,128)(2,1)}, bf16[516,512]{1,0:T(8,128)(2,1)S(1)}, u32[]{:S(2)}, u32[]{:S(2)}) collective-permute-start(bf16[516,512]{1,0:T(8,128)(2,1)} %copy-done.1), channel_id=1, source_target_pairs={{0,1},{1,0},{2,3},{3,2},{4,5},{5,4},{6,7},{7,6},{8,9},{9,8},{10,11... | collective-permute-start | bytes 1585160 | tf_op jit(solution)/shard_map/ppermute | solution.py:162
  31.7 0.8 copy-start.4
  34.0 8.9 %copy-start.9 = (f32[3,256]{1,0:T(4,128)S(1)}, f32[3,256]{1,0:T(4,128)}, u32[]{:S(2)}) copy-start(f32[3,256]{1,0:T(4,128)} %param.16) | copy-start | bytes 9220
  34.0 9.5 %copy-start.8 = (s32[4,3]{1,0:T(4,128)S(1)}, s32[4,3]{1,0:T(4,128)}, u32[]{:S(2)}) copy-start(s32[4,3]{1,0:T(4,128)} %param.20) | copy-start | bytes 148
  34.0 11.0 %copy-start.6 = (bf16[1,2,512,256]{3,2,1,0:T(8,128)(2,1)S(1)}, bf16[1,2,512,256]{3,2,1,0:T(8,128)(2,1)}, u32[]{:S(2)}) copy-start(bf16[1,2,512,256]{3,2,1,0:T(8,128)(2,1)} %param.17) | copy-start | bytes 1572868
  157.1 10.0 %copy-start.3 = (bf16[512,2,128]{2,0,1:T(8,128)(2,1)S(1)}, bf16[512,2,128]{2,0,1:T(8,128)(2,1)}, u32[]{:S(2)}) copy-start(bf16[512,2,128]{2,0,1:T(8,128)(2,1)} %copy.102) | copy-start | bytes 786436
  158.9 8.9 %copy-start.5 = (pred[512,1024]{1,0:T(8,128)(4,1)S(1)}, pred[512,1024]{1,0:T(8,128)(4,1)}, u32[]{:S(2)}) copy-start(pred[512,1024]{1,0:T(8,128)(4,1)} %pad_add_fusion) | copy-start | bytes 1572868
  161.2 11.8 %collective-permute-start.3 = (f32[4,257]{1,0:T(4,128)S(1)}, f32[4,257]{1,0:T(4,128)S(1)}, u32[]{:S(2)}, u32[]{:S(2)}) collective-permute-start(f32[4,257]{1,0:T(4,128)S(1)} %get-tuple-element.69), channel_id=1, source_target_pairs={{0,8},{8,16},{16,24},{24,32},{32,40},{40,48},{48,56},{56,64},{64,7... | collective-permute-start | bytes 12344 | tf_op jit(solution)/shard_map/ppermute | solution.py:195
  161.4 16.5 %collective-permute-start.1 = (f32[4,257]{1,0:T(4,128)S(1)}, f32[4,257]{1,0:T(4,128)S(1)}, u32[]{:S(2)}, u32[]{:S(2)}) collective-permute-start(f32[4,257]{1,0:T(4,128)S(1)} %get-tuple-element.68), channel_id=1, source_target_pairs={{8,0},{16,8},{24,16},{32,24},{40,32},{48,40},{56,48},{64,56},{72,6... | collective-permute-start | bytes 12344 | tf_op jit(solution)/shard_map/ppermute | solution.py:195
  167.8 3.1 %copy-start.2 = (bf16[4,256,2,128]{3,2,1,0:T(2,128)(2,1)S(1)}, bf16[4,256,2,128]{3,2,1,0:T(2,128)(2,1)}, u32[]{:S(2)}) copy-start(bf16[4,256,2,128]{3,2,1,0:T(2,128)(2,1)} %reshape_squeeze.28) | copy-start | bytes 1572868
  167.8 4.1 %copy-start.7 = (bf16[1,1,512,256]{2,3,1,0:T(8,128)(2,1)S(1)}, bf16[1,1,512,256]{2,3,1,0:T(8,128)(2,1)}, u32[]{:S(2)}) copy-start(bf16[1,1,512,256]{2,3,1,0:T(8,128)(2,1)} %copy.92) | copy-start | bytes 786436
  171.9 6.2 %copy-start = (bf16[4,1,1024,256]{2,3,0,1:T(8,128)(2,1)S(1)}, bf16[4,1,1024,256]{2,3,0,1:T(8,128)(2,1)}, u32[]{:S(2)}) copy-start(bf16[4,1,1024,256]{2,3,0,1:T(8,128)(2,1)} %copy.125) | copy-start | bytes 6291460
  177.7 5.0 %collective-permute-start.4 = (f32[4,2,130]{0,1,2:T(2,128)S(1)}, f32[4,2,130]{0,1,2:T(2,128)S(1)}, u32[]{:S(2)}, u32[]{:S(2)}) collective-permute-start(f32[4,2,130]{0,1,2:T(2,128)S(1)} %pad_maximum_fusion.6), channel_id=1, source_target_pairs={{8,0},{16,8},{24,16},{32,24},{40,32},{48,40},{56,48},{64,56},{72,6... | collective-permute-start | bytes 12488 | tf_op jit(solution)/shard_map/ppermute | solution.py:204
  181.0 8.4 %collective-permute-start.2 = (f32[4,2,130]{0,1,2:T(2,128)S(1)}, f32[4,2,130]{0,1,2:T(2,128)S(1)}, u32[]{:S(2)}, u32[]{:S(2)}) collective-permute-start(f32[4,2,130]{0,1,2:T(2,128)S(1)} %pad_maximum_fusion.5), channel_id=1, source_target_pairs={{0,8},{8,16},{16,24},{24,32},{32,40},{40,48},{48,56},{56,64},{64,7... | collective-permute-start | bytes 12488 | tf_op jit(solution)/shard_map/ppermute | solution.py:204
Sparse Core Ops, SparseCore 0:
  9.9 35.5 all-gather.2
  47.4 33.7 all-gather.4
where the time goes:
time: 199 us; the launch traced here: 197 us
  local copies, waits for them, and re-layouts  78.1 us (39%)
  other arithmetic  42.6 us (21%)
  waiting for transfers between devices  30.4 us (15%)
  matrix products  17.2 us (9%)
  between operations  15 us (8%)
  starting transfers between devices  13.8 us (7%)
    reduce_sum x1, other arithmetic, layer_norm(): middle = jnp.mean(rows, axis=-1, keepdims=True)  14.9 us
    ppermute x1, waiting for transfers between devices, local(): partner = lax.ppermute(rows, 'tz', [(0, 1), (1, 0)])  14.6 us
    unnamed x24, local copies, waits for them, and re-layouts  12.5 us
    reshape x1, local copies, waits for them, and re-layouts, local(): jnp.where(lower, partner_y, own_y)  12.5 us
    convert_element_type x1, local copies, waits for them, and re-layouts, layer_norm(): (centred * lax.rsqrt(spread + EPS) * gain + shift).astype(jnp.bfloat16)  10.6 us
    all_gather x1, waiting for transfers between devices, local(): partner_y = lax.all_gather(partner, 'ty', axis=1, tiled=True)  9.05 us
    convert_element_type x1, other arithmetic, layer_norm(): (centred * lax.rsqrt(spread + EPS) * gain + shift).astype(jnp.bfloat16)  8.79 us
    dot_general x1, matrix products, project(): jnp.dot(normed, weight.reshape(weight.shape[0], 3 * width), preferred_ele...  8.78 us
  transfers between devices with their start and end apart: 7, of which 3 were waited for; matrix products, arithmetic and copies ran while one was open for 27% of the time, Pallas kernels for 0%

commit v1 on v0

--- a/solution.py
+++ b/solution.py
@@ -9,6 +9,12 @@
 ROT = 32
 EPS = 1e-05
 NEG = -1e30
+
+
+def seats_all_draw(incoming_x, vector, dev_axis="ty"):
+    right_arr = jnp.concatenate([incoming_x, vector], axis=0)
+    current_block = lax.all_gather(right_arr, axis_name=dev_axis, axis=1, tiled=True)
+    return jnp.split(current_block, [incoming_x.shape[0]], axis=0)
 
 
 def with_halo(block, sides, width):
@@ -160,8 +166,7 @@
     requests = decode_x.shape[0]
     rows = jnp.concatenate([prefill_x, decode_x], axis=0)
     partner = lax.ppermute(rows, "tz", [(0, 1), (1, 0)])
-    own_y = lax.all_gather(rows, "ty", axis=1, tiled=True)
-    partner_y = lax.all_gather(partner, "ty", axis=1, tiled=True)
+    own_y, partner_y = seats_all_draw(rows, vector=partner)
     lower = lax.axis_index("tz") == 0
     first = jnp.where(lower, own_y, partner_y).reshape(rows.shape[0], -1, 1, rows.shape[1])
     second = jnp.where(lower, partner_y, own_y).reshape(rows.shape[0], -1, 1, rows.shape[1])

time: 199 us -> 216 us (1.085)
  waiting for transfers between devices: 30.4 us -> 43.6 us
  local copies, waits for them, and re-layouts: 78.1 us -> 80.8 us
    all_gather x2 -> x1, waiting for transfers between devices: 9.05 us -> 22.5 us  [seats_all_draw(): lax.all_gather(right_arr, axis_name=dev_axis, axis=1, tiled=True)]
    concatenate x1, local copies, waits for them, and re-layouts: 0.7 us -> 7.37 us  [seats_all_draw(): right_arr = jnp.concatenate([incoming_x, vector], axis=0)]
    unnamed x24 -> x23, local copies, waits for them, and re-layouts: 12.5 us -> 9.84 us
  transfers between devices with their start and end apart: 7 -> 6, of which waited for: 3 -> 3; matrix products, arithmetic and copies ran while one was open for 27% -> 24% of each run, Pallas kernels for 0% -> 0%
where the time goes in v1:
time: 216 us; the launch traced here: 214 us
  local copies, waits for them, and re-layouts  80.8 us (37%)
  other arithmetic  44.1 us (20%)
  waiting for transfers between devices  43.6 us (20%)
  matrix products  17.1 us (8%)
  between operations  15.1 us (7%)
  starting transfers between devices  13.8 us (6%)
    all_gather x1, waiting for transfers between devices, seats_all_draw(): lax.all_gather(right_arr, axis_name=dev_axis, axis=1, tiled=True)  22.5 us
    reduce_sum x1, other arithmetic, layer_norm(): middle = jnp.mean(rows, axis=-1, keepdims=True)  14.9 us
    ppermute x1, waiting for transfers between devices, local(): partner = lax.ppermute(rows, 'tz', [(0, 1), (1, 0)])  14.4 us
    reshape x1, local copies, waits for them, and re-layouts, local(): jnp.where(lower, partner_y, own_y)  12.5 us
    convert_element_type x1, local copies, waits for them, and re-layouts, layer_norm(): (centred * lax.rsqrt(spread + EPS) * gain + shift).astype(jnp.bfloat16)  10.6 us
    unnamed x23, local copies, waits for them, and re-layouts  9.84 us
    convert_element_type x1, other arithmetic, layer_norm(): (centred * lax.rsqrt(spread + EPS) * gain + shift).astype(jnp.bfloat16)  8.78 us
    dot_general x1, matrix products, project(): jnp.dot(normed, weight.reshape(weight.shape[0], 3 * width), preferred_ele...  8.76 us
  transfers between devices with their start and end apart: 6, of which 3 were waited for; matrix products, arithmetic and copies ran while one was open for 24% of the time, Pallas kernels for 0%

profile of v1, /device:TPU:8, one launch (start us, length us, event | category | flops | bytes accessed | tf_op | source)
XLA Modules:
  0.0 214.4 jit_solution(18370113637261406508)
XLA Ops:
  7.2 1.1 pad_maximum_fusion.1
  8.3 7.3 %collective-permute-start = (bf16[516,512]{1,0:T(8,128)(2,1)S(1)}, bf16[516,512]{1,0:T(8,128)(2,1)S(1)}, u32[]{:S(2)}, u32[]{:S(2)}) collective-permute-start(bf16[516,512]{1,0:T(8,128)(2,1)S(1)} %pad_maximum_fusion.1), channel_id=1, source_target_pairs={{0,1},{1,0},{2,3},{3,2},{4,5},{5,4},{6,7},{7,6},{8,9},{9,8},{10,11... | collective-permute-start | bytes 1585160 | tf_op jit(solution)/shard_map/ppermute | solution.py:168
  15.6 14.4 %collective-permute-done = bf16[516,512]{1,0:T(8,128)(2,1)S(1)} collective-permute-done((bf16[516,512]{1,0:T(8,128)(2,1)S(1)}, bf16[516,512]{1,0:T(8,128)(2,1)S(1)}, u32[]{:S(2)}, u32[]{:S(2)}) %collective-permute-start) | collective-permute-done | bytes 528416 | tf_op jit(solution)/shard_map/ppermute | solution.py:168
  30.0 7.4 %concatenate.59 = bf16[1032,512]{1,0:T(8,128)(2,1)} concatenate(bf16[512,512]{1,0:T(8,128)(2,1)} %param.11, bf16[4,512]{1,0:T(4,128)(2,1)} %param.12, bf16[516,512]{1,0:T(8,128)(2,1)S(1)} %collective-permute-done), dimensions={0} | concatenate | bytes 2113536 | tf_op jit(solution)/shard_map/concatenate | solution.py:15
  37.4 8.8 %copy.95 = bf16[4096,3,256]{0,2,1:T(8,128)(2,1)} copy(bf16[4096,3,256]{2,0,1:T(8,128)(2,1)} %param.15) | data formatting | bytes 12582912 | tf_op args[4]
  46.9 0.2 slice_convert_fusion.7
  47.2 0.2 multiply_cosine_fusion
  47.4 0.1 copy.99
  47.5 0.8 copy.98
  48.4 0.1 copy.128
  48.6 0.8 copy.102
  49.4 0.8 copy.92
  50.3 5.7 %fusion.76 = (bf16[4,1,1024,256]{3,2,1,0:T(8,128)(2,1)S(1)}, bf16[4,1,1024,256]{3,2,1,0:T(8,128)(2,1)}, bf16[4,1,1024,256]{3,2,1,0:T(8,128)(2,1)}, bf16[4,1,1024,256]{3,2,1,0:T(8,128)(2,1)}) fusion(bf16[8,2,1024,256]{3,2,1,0:T(8,128)(2,1)} %param.21), kind=kLoop, calls=%fused_computation.135 | loop fusion | bytes 16777216 | tf_op jit(solution)/shard_map/slice | solution.py:124
  56.0 4.0 %copy.126 = bf16[4,1,1024,256]{2,3,0,1:T(8,128)(2,1)} copy(bf16[4,1,1024,256]{3,2,1,0:T(8,128)(2,1)} %get-tuple-element.43) | data formatting | bytes 4194304 | tf_op jit(solution)/shard_map/reshape;squeeze | solution.py:123
  60.0 4.1 %reshape_squeeze.30 = bf16[4,1024,2,128]{3,2,1,0:T(2,128)(2,1)} reshape(bf16[4,1,1024,256]{3,2,1,0:T(8,128)(2,1)} %get-tuple-element.42) | data formatting | bytes 4194304 | tf_op jit(solution)/shard_map/reshape;squeeze | solution.py:124
  64.0 2.1 fusion.78
  66.1 1.2 reshape_squeeze.31
  67.3 1.0 reshape_squeeze.28
  68.3 4.0 %copy.125 = bf16[4,1,1024,256]{2,3,0,1:T(8,128)(2,1)} copy(bf16[4,1,1024,256]{3,2,1,0:T(8,128)(2,1)} %get-tuple-element.41) | data formatting | bytes 4194304 | tf_op jit(solution)/shard_map/reshape;squeeze | solution.py:123
  72.3 2.1 reshape_squeeze.27
  74.6 1.0 pad_add_fusion
  75.6 22.5 %all-gather.2.cloned.1.call-done = bf16[1032,2048]{1,0:T(8,128)(2,1)} async-done(((bf16[1032,512]{1,0:T(8,128)(2,1)}), bf16[1032,2048]{1,0:T(8,128)(2,1)}) %all-gather.2.cloned.1.call-update) | async-done | bytes 4227088 | tf_op jit(solution)/shard_map/all_gather | solution.py:16
  98.0 4.2 %broadcast_select_fusion.1 = (bf16[516,2048]{1,0:T(8,128)(2,1)S(1)}, bf16[516,2048]{1,0:T(8,128)(2,1)}) fusion(pred[]{:T(512)S(6)} %eq.3, bf16[1032,2048]{1,0:T(8,128)(2,1)} %all-gather.2.cloned.1.call-done), kind=kLoop, calls=%fused_computation.14 | loop fusion | flops 2113536 | bytes 8454145 | tf_op jit(solution)/shard_map/jit(_where)/select_n | solution.py:171
  102.3 12.5 %reshape.299 = bf16[516,4,1,512]{3,2,1,0:T(2,128)(2,1)} reshape(bf16[516,2048]{1,0:T(8,128)(2,1)} %get-tuple-element.45) | data formatting | bytes 4227072 | tf_op jit(solution)/shard_map/reshape | solution.py:172
  114.8 5.5 %reshape.298 = bf16[516,4,1,512]{3,2,1,0:T(2,128)(2,1)} reshape(bf16[516,2048]{1,0:T(8,128)(2,1)S(1)} %get-tuple-element.44) | data formatting | bytes 4227072 | tf_op jit(solution)/shard_map/reshape | solution.py:171
  120.3 14.9 %convert_reduce_fusion = (f32[516]{0:T(1024)S(1)}, bf16[516,4,2,512]{3,2,1,0:T(2,128)(2,1)S(1)}) fusion(bf16[516,4,1,512]{3,2,1,0:T(2,128)(2,1)} %reshape.299, bf16[516,4,1,512]{3,2,1,0:T(2,128)(2,1)} %reshape.298), kind=kLoop, calls=%fused_computation.2 | loop fusion | flops 12680700 | bytes 8456208 | tf_op jit(solution)/shard_map/reduce_sum | solution.py:36
  135.1 6.1 %fusion.3 = f32[516]{0:T(1024)S(1)} fusion(bf16[516,4,2,512]{3,2,1,0:T(2,128)(2,1)S(1)} %get-tuple-element.39, f32[516]{0:T(1024)S(1)} %broadcast_multiply_fusion), kind=kLoop, calls=%fused_computation.5 | loop fusion | flops 8453628 | bytes 4231200 | tf_op jit(solution)/shard_map/reduce_sum | solution.py:38
  141.3 8.8 %fusion.6 = bf16[516,4,2,512]{3,2,1,0:T(2,128)(2,1)} fusion(bf16[516,4,2,512]{3,2,1,0:T(2,128)(2,1)S(1)} %get-tuple-element.39, f32[516]{0:T(1024)S(1)} %add_rsqrt_fusion, f32[516]{0:T(1024)S(1)} %broadcast_multiply_fusion, f32[4,2,512]{2,1,0:T(2,128)S(1)} %add.81, f32[4,2,512]{2,1,0:T(2,128)S(1)} %mul.188), kind=kLoop, calls=%fused_computation.8 | loop fusion | flops 12681216 | bytes 8491040 | tf_op jit(solution)/shard_map/convert_element_type | solution.py:39
  150.0 10.6 %convert_element_type.82 = bf16[516,4096]{1,0:T(8,128)(2,1)} reshape(bf16[516,4,2,512]{3,2,1,0:T(2,128)(2,1)} %fusion.6) | data formatting | bytes 8454144 | tf_op jit(solution)/shard_map/convert_element_type | solution.py:39
  160.6 8.8 %convolution_add_fusion = f32[516,768]{1,0:T(8,128)} fusion(bf16[516,4096]{1,0:T(8,128)(2,1)} %convert_element_type.82, bf16[4096,768]{0,1:T(8,128)(2,1)} %bitcast.118, f32[768]{0:T(1024)S(1)} %add.84), kind=kOutput, calls=%fused_computation.25 | convolution fusion | flops 3246787584 | bytes 12106752 | tf_op jit(solution)/shard_map/dot_general | solution.py:60
  169.4 2.1 reshape.279
  171.5 0.4 fusion.77
  171.8 2.2 %copy.96 = bf16[516,3,2,128]{0,3,2,1:T(8,128)(2,1)} copy(f32[516,3,2,128]{3,2,1,0:T(2,128)S(1)} %reshape.279) | data formatting | bytes 2377728 | tf_op jit(solution)/shard_map/reshape | solution.py:63
  174.1 0.1 slice.249
  174.3 0.1 slice.250
  174.4 1.4 subtract_convert_fusion.1
  175.9 0.3 pad_maximum_fusion.4
  176.2 1.0 slice_bitcast_fusion
  177.3 0.8 slice.182
  178.1 0.3 pad_maximum_fusion.5
  178.7 5.7 %collective-permute-start.1 = (f32[4,257]{1,0:T(4,128)S(1)}, f32[4,257]{1,0:T(4,128)S(1)}, u32[]{:S(2)}, u32[]{:S(2)}) collective-permute-start(f32[4,257]{1,0:T(4,128)S(1)} %get-tuple-element.68), channel_id=1, source_target_pairs={{8,0},{16,8},{24,16},{32,24},{40,32},{48,40},{56,48},{64,56},{72,6... | collective-permute-start | bytes 12344 | tf_op jit(solution)/shard_map/ppermute | solution.py:200
  184.4 0.7 fusion.33
  185.1 2.4 %fusion.80 = (f32[2,512]{1,0:T(2,128)S(1)}, bf16[2,512,1024]{2,1,0:T(8,128)(2,1)S(1)}) fusion(f32[2,512,1024]{2,1,0:T(8,128)S(1)} %fusion.33, pred[512,1024]{1,0:T(8,128)(4,1)S(1)} %copy-done.3), kind=kOutput, calls=%fused_computation.139 | output fusion | flops 8389631 | bytes 6819840 | tf_op jit(solution)/shard_map/while/body/eval_jaxpr/sub | solution.py:76
  187.5 0.7 pad_maximum_fusion.3
  188.2 0.7 pad_maximum_fusion.2
  188.9 0.3 fusion.28
  189.2 0.8 fusion.23
  190.1 0.2 fusion.56
  190.5 2.0 fusion.82
  192.5 0.2 fusion.50
  192.7 2.0 fusion.8
  194.7 0.2 copy.121
  195.0 0.2 collective-permute-start.4
  195.4 0.4 fusion.81
  195.9 0.2 fusion.51
  196.1 2.0 fusion.10
  198.1 0.2 copy.112
  198.3 0.4 collective-permute-start.2
  198.8 0.2 fusion.26
  199.0 0.9 copy.106
  199.8 0.2 copy.124
  200.0 6.7 %collective-permute-done.2 = f32[4,2,130]{0,1,2:T(2,128)S(1)} collective-permute-done((f32[4,2,130]{0,1,2:T(2,128)S(1)}, f32[4,2,130]{0,1,2:T(2,128)S(1)}, u32[]{:S(2)}, u32[]{:S(2)}) %collective-permute-start.2) | collective-permute-done | bytes 4192 | tf_op jit(solution)/shard_map/ppermute | solution.py:209
  206.8 0.1 fusion.41
  206.9 0.7 copy.105
  (62 shorter events, 1.7 us)
Async XLA Ops:
  7.2 30.2 %copy-start.7 = (f32[4096]{0:T(1024)S(1)}, f32[4096]{0:T(1024)}, u32[]{:S(2)}) copy-start(f32[4096]{0:T(1024)} %param.14) | copy-start | bytes 49156
  7.2 30.2 %copy-start.8 = (f32[4096]{0:T(1024)S(1)}, f32[4096]{0:T(1024)}, u32[]{:S(2)}) copy-start(f32[4096]{0:T(1024)} %param.13) | copy-start | bytes 49156
  7.2 90.8 %all-gather.2.cloned.1.call-start = ((), (), s32[]{:S(2)}) async-start(), calls=%async_computation | async-start | bytes 5283840 | tf_op jit(solution)/shard_map/all_gather | solution.py:16
  8.3 21.6 %collective-permute-start = (bf16[516,512]{1,0:T(8,128)(2,1)S(1)}, bf16[516,512]{1,0:T(8,128)(2,1)S(1)}, u32[]{:S(2)}, u32[]{:S(2)}) collective-permute-start(bf16[516,512]{1,0:T(8,128)(2,1)S(1)} %pad_maximum_fusion.1), channel_id=1, source_target_pairs={{0,1},{1,0},{2,3},{3,2},{4,5},{5,4},{6,7},{7,6},{8,9},{9,8},{10,11... | collective-permute-start | bytes 1585160 | tf_op jit(solution)/shard_map/ppermute | solution.py:168
  37.4 8.8 %copy-start.9 = (f32[3,256]{1,0:T(4,128)S(1)}, f32[3,256]{1,0:T(4,128)}, u32[]{:S(2)}) copy-start(f32[3,256]{1,0:T(4,128)} %param.16) | copy-start | bytes 9220
  37.4 9.5 %copy-start.6 = (s32[4,3]{1,0:T(4,128)S(1)}, s32[4,3]{1,0:T(4,128)}, u32[]{:S(2)}) copy-start(s32[4,3]{1,0:T(4,128)} %param.20) | copy-start | bytes 148
  37.4 11.0 %copy-start.4 = (bf16[1,2,512,256]{3,2,1,0:T(8,128)(2,1)S(1)}, bf16[1,2,512,256]{3,2,1,0:T(8,128)(2,1)}, u32[]{:S(2)}) copy-start(bf16[1,2,512,256]{3,2,1,0:T(8,128)(2,1)} %param.17) | copy-start | bytes 1572868
  174.4 10.0 %copy-start.2 = (bf16[512,2,128]{2,0,1:T(8,128)(2,1)S(1)}, bf16[512,2,128]{2,0,1:T(8,128)(2,1)}, u32[]{:S(2)}) copy-start(bf16[512,2,128]{2,0,1:T(8,128)(2,1)} %copy.102) | copy-start | bytes 786436
  176.2 8.9 %copy-start.3 = (pred[512,1024]{1,0:T(8,128)(4,1)S(1)}, pred[512,1024]{1,0:T(8,128)(4,1)}, u32[]{:S(2)}) copy-start(pred[512,1024]{1,0:T(8,128)(4,1)} %pad_add_fusion) | copy-start | bytes 1572868
  178.5 11.8 %collective-permute-start.3 = (f32[4,257]{1,0:T(4,128)S(1)}, f32[4,257]{1,0:T(4,128)S(1)}, u32[]{:S(2)}, u32[]{:S(2)}) collective-permute-start(f32[4,257]{1,0:T(4,128)S(1)} %get-tuple-element.69), channel_id=1, source_target_pairs={{0,8},{8,16},{16,24},{24,32},{32,40},{40,48},{48,56},{56,64},{64,7... | collective-permute-start | bytes 12344 | tf_op jit(solution)/shard_map/ppermute | solution.py:200
  178.7 16.5 %collective-permute-start.1 = (f32[4,257]{1,0:T(4,128)S(1)}, f32[4,257]{1,0:T(4,128)S(1)}, u32[]{:S(2)}, u32[]{:S(2)}) collective-permute-start(f32[4,257]{1,0:T(4,128)S(1)} %get-tuple-element.68), channel_id=1, source_target_pairs={{8,0},{16,8},{24,16},{32,24},{40,32},{48,40},{56,48},{64,56},{72,6... | collective-permute-start | bytes 12344 | tf_op jit(solution)/shard_map/ppermute | solution.py:200
  185.1 3.1 %copy-start.1 = (bf16[4,256,2,128]{3,2,1,0:T(2,128)(2,1)S(1)}, bf16[4,256,2,128]{3,2,1,0:T(2,128)(2,1)}, u32[]{:S(2)}) copy-start(bf16[4,256,2,128]{3,2,1,0:T(2,128)(2,1)} %reshape_squeeze.28) | copy-start | bytes 1572868
  185.1 4.1 %copy-start.5 = (bf16[1,1,512,256]{2,3,1,0:T(8,128)(2,1)S(1)}, bf16[1,1,512,256]{2,3,1,0:T(8,128)(2,1)}, u32[]{:S(2)}) copy-start(bf16[1,1,512,256]{2,3,1,0:T(8,128)(2,1)} %copy.92) | copy-start | bytes 786436
  189.2 6.2 %copy-start = (bf16[4,1,1024,256]{2,3,0,1:T(8,128)(2,1)S(1)}, bf16[4,1,1024,256]{2,3,0,1:T(8,128)(2,1)}, u32[]{:S(2)}) copy-start(bf16[4,1,1024,256]{2,3,0,1:T(8,128)(2,1)} %copy.125) | copy-start | bytes 6291460
  195.0 5.0 %collective-permute-start.4 = (f32[4,2,130]{0,1,2:T(2,128)S(1)}, f32[4,2,130]{0,1,2:T(2,128)S(1)}, u32[]{:S(2)}, u32[]{:S(2)}) collective-permute-start(f32[4,2,130]{0,1,2:T(2,128)S(1)} %pad_maximum_fusion.7), channel_id=1, source_target_pairs={{8,0},{16,8},{24,16},{32,24},{40,32},{48,40},{56,48},{64,56},{72,6... | collective-permute-start | bytes 12488 | tf_op jit(solution)/shard_map/ppermute | solution.py:209
  198.3 8.4 %collective-permute-start.2 = (f32[4,2,130]{0,1,2:T(2,128)S(1)}, f32[4,2,130]{0,1,2:T(2,128)S(1)}, u32[]{:S(2)}, u32[]{:S(2)}) collective-permute-start(f32[4,2,130]{0,1,2:T(2,128)S(1)} %pad_maximum_fusion.6), channel_id=1, source_target_pairs={{0,8},{8,16},{16,24},{24,32},{32,40},{40,48},{48,56},{56,64},{64,7... | collective-permute-start | bytes 12488 | tf_op jit(solution)/shard_map/ppermute | solution.py:209
Sparse Core Ops, SparseCore 0:
  37.5 60.5 all-gather.1
